TPU v7x, 32 devices: a whole 2x2x4 slice. The times are simulated.
32 devices in a mesh: row: 8 (over z, y), col: 4 (over x, core).
Axes of the slice: x: 2, y: 2, z: 4, core: 2. Of those that a mesh axis runs over, the one named last changes fastest.
Arguments:
- gram: float32 [16384, 16384], P('row', 'col'), may hold values from -1 to 17, as said below
Outputs:
- factored: float32 [16384, 16384], P('row', 'col')
Inputs may be any that keep to these rules, and one draw needn't show every extreme that they name: gram holds a symmetric positive definite matrix in the block-cyclic order of the steps.
All inputs are finite; a program needn't handle non-finite values.
Results may differ from a plain program's by a relative error of at most 0.0001.
Values sent between devices are 32-bit elements; how exact they have to be, the bound alone decides.
No kernel may reach another device: no remote copies, remote signals or barrier semaphores. Data moves between devices by JAX's collectives and lax.ppermute only.
A program may use at most 192 MiB of HBM per device.

v0:
```python
import jax
import jax.numpy as jnp
from jax import lax
from jax.sharding import PartitionSpec as P

NB = 512
STEPS = 2


def broadcast(value, axis, source):
    kept = jnp.where(lax.axis_index(axis) == source, value, 0).astype(value.dtype)
    return lax.psum(kept, axis)


def from_partner(block, axis, apart):
    count = lax.axis_size(axis)
    route = []
    for low in range(count):
        high = low | 1 << apart
        if high != low and high < count:
            route += [(low, high), (high, low)]
    return lax.ppermute(block, axis, route)


def global_index(count, block, grid, position):
    ladder = jnp.arange(count, dtype=jnp.int32)
    return (ladder // block * grid + position) * block + ladder % block


def times_transposed(left, right):
    return lax.dot_general(
        left,
        right,
        (((1,), (1,)), ((), ())),
        precision=lax.Precision.HIGHEST,
        preferred_element_type=jnp.float32,
    )


def local(gram):
    grid_rows = lax.axis_size("row")
    grid_cols = lax.axis_size("col")
    row_id = lax.axis_index("row")
    col_id = lax.axis_index("col")
    rblock = NB * grid_cols // grid_rows
    per_class = grid_rows // grid_cols
    local_rows = gram.shape[0]
    local_cols = gram.shape[1]
    blocks = local_rows // rblock
    grows = global_index(local_rows, rblock, grid_rows, row_id)
    gcols = global_index(local_cols, NB, grid_cols, col_id)
    member = row_id % per_class
    row_class = row_id // per_class
    identity = jnp.eye(NB, dtype=jnp.float32)

    def factor_panel(matrix, panel_index):
        owner_col = panel_index % grid_cols
        local_block = panel_index // grid_cols
        end_row = panel_index * NB + NB
        column = matrix[:, local_block * NB : (local_block + 1) * NB]
        square = column[local_block * rblock : (local_block + 1) * rblock]
        is_owner = col_id == owner_col
        in_class = row_class == owner_col
        select = (jnp.arange(per_class, dtype=jnp.int32) == member).astype(jnp.float32)
        weight = jnp.where(is_owner & in_class, 1.0, 0.0).astype(jnp.float32)
        placed = (select[:, None, None] * square[None]).reshape(NB, NB) * weight
        diagonal = lax.psum(placed, "row")
        diagonal = jnp.where(is_owner, diagonal, identity)
        low_factor = jnp.linalg.cholesky(diagonal)
        inverse = jax.scipy.linalg.solve_triangular(low_factor, identity, lower=True)
        solved = times_transposed(column, inverse)
        trailing = jnp.where((grows >= end_row)[:, None], solved, 0.0)
        rows_diag = lax.dynamic_slice_in_dim(low_factor, member * rblock, rblock, 0)
        previous = trailing[local_block * rblock : (local_block + 1) * rblock]
        patched = jnp.where(in_class, rows_diag, previous)
        factored = trailing.at[local_block * rblock : (local_block + 1) * rblock].set(patched)
        new_column = jnp.where(is_owner, factored, column)
        matrix = matrix.at[:, local_block * NB : (local_block + 1) * NB].set(new_column)
        return (matrix, trailing)

    matrix = gram
    for panel_index in range(STEPS):
        matrix, trailing = factor_panel(matrix, panel_index)
        spread_owner_col = panel_index % grid_cols
        spread_rows_all = broadcast(trailing, "col", spread_owner_col)
        pieces = spread_rows_all.reshape(grid_cols, blocks // grid_cols * rblock, NB)
        shift_bits = per_class.bit_length() - 1
        for bit_level in reversed(range(grid_cols.bit_length() - 1)):
            halfway = pieces.shape[0] // 2
            own_bit = row_class >> bit_level & 1
            wanted = col_id >> bit_level & 1
            upper = own_bit == 1
            retained = jnp.where(upper, pieces[halfway:], pieces[:halfway])
            outgoing = jnp.where(upper, pieces[:halfway], pieces[halfway:])
            received = from_partner(outgoing, "row", shift_bits + bit_level)
            pieces = jnp.where(own_bit == wanted, retained, received)
        gathered = lax.all_gather(pieces[0], "row", axis=0, tiled=True)
        spread_columns = gathered.reshape(grid_cols, per_class, blocks // grid_cols, rblock, NB)
        spread_columns = jnp.transpose(spread_columns, (0, 2, 1, 3, 4)).reshape(local_cols, NB)
        first_row = panel_index * NB
        apply_end_row = first_row + NB
        current = matrix
        updated = current - times_transposed(spread_rows_all, spread_columns)
        panel_rows = (grows >= first_row) & (grows < apply_end_row)
        beyond = gcols >= apply_end_row
        updated = jnp.where(panel_rows[:, None] & beyond[None, :], 0.0, updated)
        matrix = matrix.at[:, 0:local_cols].set(updated)
    matrix, trailing = factor_panel(matrix, STEPS)
    return matrix


def solution(mesh):
    placed = (P("row", "col"),)
    return jax.shard_map(
        local, mesh=mesh, in_specs=placed, out_specs=P("row", "col"), check_vma=False
    )
```

profile of v0, /device:TPU:0, one launch (start us, length us, event | category | flops | bytes accessed | tf_op | source)
XLA Modules:
  0.0 1543.9 jit_solution(489001765417519902)
XLA Ops:
  6.5 23.0 %copy.106 = f32[2048,4096]{1,0:T(8,128)} copy(f32[2048,4096]{1,0:T(8,128)} %param.24) | data formatting | bytes 67108864
  32.8 81.1 %all-reduce.7.cloned.1.call-done = f32[512,512]{0,1:T(8,128)} async-done(((f32[512,512]{0,1:T(8,128)}), f32[512,512]{0,1:T(8,128)}) %all-reduce.7.cloned.1.call-update) | async-done | bytes 1048592 | tf_op jit(solution)/shard_map/psum | solution.py:67
  118.1 11.7 cholesky.374
  130.0 9.8 custom-call.31
  140.5 11.7 cholesky.393
  152.3 10.0 custom-call.32
  162.9 11.7 cholesky.414
  174.6 9.8 custom-call.33
  185.1 11.7 cholesky.431
  203.0 8.4 while.16
  211.4 39.3 %custom-call.34 = f32[4,128,128]{1,2,0:T(8,128)S(1)} custom-call(f32[4,128,128]{2,1,0:T(8,128)S(1)} %get-tuple-element.139), custom_call_target="InvertDiagBlocksLowerTriangular" | custom-call | tf_op jit(solution)/shard_map/jit(_solve_triangular)/triangular_solve | solution.py:70
  255.5 10.6 broadcast_select_fusion.1
  266.2 84.3 %all-reduce.9.cloned.1.call-done = f32[2048,512]{1,0:T(8,128)} async-done(((f32[2048,512]{1,0:T(8,128)}), f32[2048,512]{1,0:T(8,128)}) %all-reduce.9.cloned.1.call-update) | async-done | bytes 4194320 | tf_op jit(solution)/shard_map/psum | solution.py:12
  350.5 4.8 slice_select_fusion.2
  357.7 90.7 %collective-permute-done = f32[2,512,512]{2,1,0:T(8,128)S(1)} collective-permute-done((f32[2,512,512]{2,1,0:T(8,128)}, f32[2,512,512]{2,1,0:T(8,128)S(1)}, u32[]{:S(2)}, u32[]{:S(2)}) %collective-permute-start) | collective-permute-done | bytes 2097184 | tf_op jit(solution)/shard_map/ppermute | solution.py:22
  453.6 23.9 %collective-permute-done.1 = f32[1,512,512]{2,1,0:T(8,128)} collective-permute-done((f32[1,512,512]{2,1,0:T(8,128)}, f32[1,512,512]{2,1,0:T(8,128)}, u32[]{:S(2)}, u32[]{:S(2)}) %collective-permute-start.1) | collective-permute-done | bytes 1048608 | tf_op jit(solution)/shard_map/ppermute | solution.py:22
  482.2 7.1 fusion
  489.3 116.8 %all-gather.5.cloned.1.call-done = f32[1,4096,512]{2,1,0:T(8,128)} async-done(((f32[1,512,512]{2,1,0:T(8,128)}), f32[1,4096,512]{2,1,0:T(8,128)}) %all-gather.5.cloned.1.call-update) | async-done | bytes 8388624 | tf_op jit(solution)/shard_map/all_gather | solution.py:97
  610.7 60.7 %subtract_select_fusion.1 = f32[2048,4096]{1,0:T(8,128)} fusion(f32[2048,4096]{1,0:T(8,128)} %fusion, pred[4096]{0:T(1024)(128)(4,1)S(1)} %broadcast_compare_fusion.1, pred[2048]{0:T(1024)(128)(4,1)S(1)} %get-tuple-element.222, f32[2048,512]{1,0:T(8,128)S(1)} %copy-done, f32[4096,512]{1,0:T(8,128)S(1)} %bitcast.177), kind=kOutput, calls=%fused_computation.7 | convolution fusion | flops 51564773376 | bytes 79697920 | tf_op jit(solution)/shard_map/dot_general | solution.py:31
  674.6 76.4 %all-reduce.11.cloned.1.call-done = f32[512,512]{0,1:T(8,128)} async-done(((f32[512,512]{0,1:T(8,128)}), f32[512,512]{0,1:T(8,128)}) %all-reduce.11.cloned.1.call-update) | async-done | bytes 1048592 | tf_op jit(solution)/shard_map/psum | solution.py:67
  754.0 11.7 cholesky.446
  765.9 9.8 custom-call.35
  776.4 11.7 cholesky.465
  788.1 10.0 custom-call.36
  798.8 11.7 cholesky.486
  810.6 9.8 custom-call.37
  821.0 11.7 cholesky.503
  839.8 8.4 while.17
  848.2 39.3 %custom-call.38 = f32[4,128,128]{1,2,0:T(8,128)S(1)} custom-call(f32[4,128,128]{2,1,0:T(8,128)S(1)} %get-tuple-element.140), custom_call_target="InvertDiagBlocksLowerTriangular" | custom-call | tf_op jit(solution)/shard_map/jit(_solve_triangular)/triangular_solve | solution.py:70
  892.3 10.6 broadcast_select_fusion
  903.1 85.0 %all-reduce.13.cloned.1.call-done = f32[2048,512]{1,0:T(8,128)} async-done(((f32[2048,512]{1,0:T(8,128)}), f32[2048,512]{1,0:T(8,128)}) %all-reduce.13.cloned.1.call-update) | async-done | bytes 4194320 | tf_op jit(solution)/shard_map/psum | solution.py:12
  993.4 90.5 %collective-permute-done.2 = f32[2,512,512]{2,1,0:T(8,128)S(1)} collective-permute-done((f32[2,512,512]{2,1,0:T(8,128)S(1)}, f32[2,512,512]{2,1,0:T(8,128)S(1)}, u32[]{:S(2)}, u32[]{:S(2)}) %collective-permute-start.2) | collective-permute-done | bytes 2097184 | tf_op jit(solution)/shard_map/ppermute | solution.py:22
  1085.1 23.7 %collective-permute-done.3 = f32[1,512,512]{2,1,0:T(8,128)S(1)} collective-permute-done((f32[1,512,512]{2,1,0:T(8,128)S(1)}, f32[1,512,512]{2,1,0:T(8,128)S(1)}, u32[]{:S(2)}, u32[]{:S(2)}) %collective-permute-start.3) | collective-permute-done | bytes 1048608 | tf_op jit(solution)/shard_map/ppermute | solution.py:22
  1112.3 5.8 fusion.1
  1118.1 118.1 %all-gather.7.cloned.1.call-done = f32[1,4096,512]{2,1,0:T(8,128)} async-done(((f32[1,512,512]{2,1,0:T(8,128)}), f32[1,4096,512]{2,1,0:T(8,128)}) %all-gather.7.cloned.1.call-update) | async-done | bytes 8388624 | tf_op jit(solution)/shard_map/all_gather | solution.py:97
  1240.8 60.9 %subtract_select_fusion = f32[2048,4096]{1,0:T(8,128)} fusion(f32[2048,4096]{1,0:T(8,128)} %fusion.1, pred[4096]{0:T(1024)(128)(4,1)S(1)} %broadcast_compare_fusion, pred[2048]{0:T(1024)(128)(4,1)S(1)} %compare_and_fusion.1, f32[2048,512]{1,0:T(8,128)S(1)} %copy-done.1, f32[4096,512]{1,0:T(8,128)S(1)} %bitcast.178), kind=kOutput, calls=%fused_computation.6 | convolution fusion | flops 51564773376 | bytes 79697920 | tf_op jit(solution)/shard_map/dot_general | solution.py:31
  1304.6 76.6 %all-reduce.15.cloned.1.call-done = f32[512,512]{0,1:T(8,128)} async-done(((f32[512,512]{0,1:T(8,128)}), f32[512,512]{0,1:T(8,128)}) %all-reduce.15.cloned.1.call-update) | async-done | bytes 1048592 | tf_op jit(solution)/shard_map/psum | solution.py:67
  1384.3 11.7 cholesky.518
  1396.1 9.8 custom-call.39
  1406.6 11.7 cholesky.537
  1418.4 10.2 custom-call.40
  1429.3 11.7 cholesky.558
  1441.0 9.8 custom-call.41
  1451.4 11.9 cholesky.575
  1469.8 8.1 while.18
  1478.0 39.3 %custom-call.42 = f32[4,128,128]{1,2,0:T(8,128)S(1)} custom-call(f32[4,128,128]{2,1,0:T(8,128)S(1)} %get-tuple-element.141), custom_call_target="InvertDiagBlocksLowerTriangular" | custom-call | tf_op jit(solution)/shard_map/jit(_solve_triangular)/triangular_solve | solution.py:70
  1522.1 8.7 fusion.14
  1531.0 5.8 fusion.2
  (199 shorter events, 108.4 us)
Async XLA Ops:
  6.5 107.3 %all-reduce.7.cloned.1.call-start = ((), (), s32[]{:S(2)}) async-start(), calls=%async_computation | async-start | bytes 2097152 | tf_op jit(solution)/shard_map/psum | solution.py:67
  32.6 317.9 %all-reduce.9.cloned.1.call-start = ((), (), s32[]{:S(2)}) async-start(), calls=%async_computation.1 | async-start | bytes 8388608 | tf_op jit(solution)/shard_map/psum | solution.py:12
  113.9 2.8 copy-start.2
  266.2 340.0 %all-gather.5.cloned.1.call-start = ((), (), s32[]{:S(2)}) async-start(), calls=%async_computation.5 | async-start | bytes 9437184 | tf_op jit(solution)/shard_map/all_gather | solution.py:97
  355.3 93.1 %collective-permute-start = (f32[2,512,512]{2,1,0:T(8,128)}, f32[2,512,512]{2,1,0:T(8,128)S(1)}, u32[]{:S(2)}, u32[]{:S(2)}) collective-permute-start(f32[2,512,512]{2,1,0:T(8,128)} %bitcast.13), channel_id=1, source_target_pairs={{0,16},{16,0},{4,20},{20,4},{8,24},{24,8},{12,28},{28,12},{1,17},{... | collective-permute-start | bytes 6291464 | tf_op jit(solution)/shard_map/ppermute | solution.py:22
  448.4 1.3 copy-start.7
  453.0 24.5 %collective-permute-start.1 = (f32[1,512,512]{2,1,0:T(8,128)}, f32[1,512,512]{2,1,0:T(8,128)}, u32[]{:S(2)}, u32[]{:S(2)}) collective-permute-start(f32[1,512,512]{2,1,0:T(8,128)} %slice_select_fusion.5), channel_id=1, source_target_pairs={{0,8},{8,0},{4,12},{12,4},{16,24},{24,16},{20,28},{28,20},{1,9},{9... | collective-permute-start | bytes 3145736 | tf_op jit(solution)/shard_map/ppermute | solution.py:22
  478.9 272.1 %all-reduce.11.cloned.1.call-start = ((), (), s32[]{:S(2)}) async-start(), calls=%async_computation.2 | async-start | bytes 2097152 | tf_op jit(solution)/shard_map/psum | solution.py:67
  606.1 4.6 copy-start
  674.4 313.7 %all-reduce.13.cloned.1.call-start = ((), (), s32[]{:S(2)}) async-start(), calls=%async_computation.3 | async-start | bytes 8388608 | tf_op jit(solution)/shard_map/psum | solution.py:12
  751.0 1.5 copy-start.3
  902.9 333.3 %all-gather.7.cloned.1.call-start = ((), (), s32[]{:S(2)}) async-start(), calls=%async_computation.6 | async-start | bytes 9437184 | tf_op jit(solution)/shard_map/all_gather | solution.py:97
  990.9 93.0 %collective-permute-start.2 = (f32[2,512,512]{2,1,0:T(8,128)S(1)}, f32[2,512,512]{2,1,0:T(8,128)S(1)}, u32[]{:S(2)}, u32[]{:S(2)}) collective-permute-start(f32[2,512,512]{2,1,0:T(8,128)S(1)} %bitcast.189), channel_id=1, source_target_pairs={{0,16},{16,0},{4,20},{20,4},{8,24},{24,8},{12,28},{28,12},{1,17},{... | collective-permute-start | bytes 6291464 | tf_op jit(solution)/shard_map/ppermute | solution.py:22
  1084.3 26.0 %copy-start.5 = (f32[512,512]{1,0:T(8,128)S(1)}, f32[512,512]{1,0:T(8,128)}, u32[]{:S(2)}) copy-start(f32[512,512]{1,0:T(8,128)} %get-tuple-element.169) | copy-start | bytes 3145732
  1084.6 24.2 %collective-permute-start.3 = (f32[1,512,512]{2,1,0:T(8,128)S(1)}, f32[1,512,512]{2,1,0:T(8,128)S(1)}, u32[]{:S(2)}, u32[]{:S(2)}) collective-permute-start(f32[1,512,512]{2,1,0:T(8,128)S(1)} %slice_select_fusion.4), channel_id=1, source_target_pairs={{0,8},{8,0},{4,12},{12,4},{16,24},{24,16},{20,28},{28,20},{1,9},{9... | collective-permute-start | bytes 3145736 | tf_op jit(solution)/shard_map/ppermute | solution.py:22
  1110.2 271.1 %all-reduce.15.cloned.1.call-start = ((), (), s32[]{:S(2)}) async-start(), calls=%async_computation.4 | async-start | bytes 2097152 | tf_op jit(solution)/shard_map/psum | solution.py:67
  1236.2 4.6 copy-start.1
  1381.3 1.5 copy-start.4
  1522.1 8.7 copy-start.6
Sparse Core Ops, SparseCore 0:
  32.7 81.0 all-reduce.6
  266.3 84.1 all-reduce.8
  479.1 127.0 all-gather.4
  674.5 76.4 all-reduce.10
  903.0 85.0 all-reduce.12
  1110.3 125.8 all-gather.6
  1304.7 76.4 all-reduce.14
where the time goes:
time: 1550 us; the launch traced here: 1540 us
  waiting for transfers between devices  867 us (56%)
  other arithmetic  408 us (26%)
  matrix products  171 us (11%)
  local copies, waits for them, and re-layouts  67.9 us (4%)
  between operations  22.3 us (1%)
    another operation x44, other arithmetic, factor_panel(): low_factor = jnp.linalg.cholesky(diagonal)  238 us
    all_gather x2, waiting for transfers between devices, local(): gathered = lax.all_gather(pieces[0], 'row', axis=0, tiled=True)  235 us
    psum x3, waiting for transfers between devices, factor_panel(): diagonal = lax.psum(placed, 'row')  234 us
    ppermute x4, waiting for transfers between devices, from_partner(): return lax.ppermute(block, axis, route)  229 us
    psum x2, waiting for transfers between devices, broadcast(): return lax.psum(kept, axis)  169 us
    dot_general x5, matrix products, times_transposed(): lax.dot_general(left, right, (((1,), (1,)), ((), ())), precision=lax.Prec...  152 us
    another operation x7, other arithmetic, factor_panel(): jax.scipy.linalg.solve_triangular(low_factor, identity, lower=True)  122 us
  transfers between devices with their start and end apart: 11, of which 11 were waited for; matrix products, arithmetic and copies ran while one was open for 1% of the time, Pallas kernels for 0%

commit v1 on v0

--- a/solution.py
+++ b/solution.py
@@ -5,6 +5,18 @@
 
 NB = 512
 STEPS = 2
+
+
+def _press_groups(inner_x, mesh_name):
+    s_next, y_new = (lax.axis_size(mesh_name), lax.axis_index(mesh_name))
+    f_next, v_now = (inner_x, 1)
+    while v_now < s_next:
+        p_next = lax.ppermute(f_next, mesh_name, [(m, m ^ v_now) for m in range(s_next)])
+        z1 = jnp.concatenate([f_next, p_next], axis=0)
+        r_now = jnp.concatenate([p_next, f_next], axis=0)
+        f_next = jnp.where(y_new & v_now == 0, z1, r_now)
+        v_now = 2 * v_now
+    return f_next
 
 
 def broadcast(value, axis, source):
@@ -94,7 +106,7 @@
             outgoing = jnp.where(upper, pieces[:halfway], pieces[halfway:])
             received = from_partner(outgoing, "row", shift_bits + bit_level)
             pieces = jnp.where(own_bit == wanted, retained, received)
-        gathered = lax.all_gather(pieces[0], "row", axis=0, tiled=True)
+        gathered = _press_groups(pieces[0], "row")
         spread_columns = gathered.reshape(grid_cols, per_class, blocks // grid_cols, rblock, NB)
         spread_columns = jnp.transpose(spread_columns, (0, 2, 1, 3, 4)).reshape(local_cols, NB)
         first_row = panel_index * NB

time: 1550 us -> 1840 us (1.19)
  waiting for transfers between devices: 867 us -> 1110 us
  other arithmetic: 408 us -> 441 us
    ppermute x0 -> x6, waiting for transfers between devices: none -> 474 us  [_press_groups(): lax.ppermute(f_next, mesh_name, [(m, m ^ v_now) for m in range(s_next)])]
    all_gather x2 -> x0, waiting for transfers between devices: 235 us -> none  [local(): gathered = lax.all_gather(pieces[0], 'row', axis=0, tiled=True)]
    select_n x0 -> x6, other arithmetic: none -> 24 us  [_press_groups(): f_next = jnp.where(y_new & v_now == 0, z1, r_now)]
  transfers between devices with their start and end apart: 11 -> 15, of which waited for: 11 -> 15; matrix products, arithmetic and copies ran while one was open for 1% -> 1% of each run, Pallas kernels for 0% -> 0%
where the time goes in v1:
time: 1840 us; the launch traced here: 1830 us
  waiting for transfers between devices  1110 us (60%)
  other arithmetic  441 us (24%)
  matrix products  172 us (9%)
  local copies, waits for them, and re-layouts  62.6 us (3%)
  starting transfers between devices  22.7 us (1%)
  between operations  22 us (1%)
    ppermute x6, waiting for transfers between devices, _press_groups(): lax.ppermute(f_next, mesh_name, [(m, m ^ v_now) for m in range(s_next)])  474 us
    another operation x44, other arithmetic, factor_panel(): low_factor = jnp.linalg.cholesky(diagonal)  248 us
    psum x3, waiting for transfers between devices, factor_panel(): diagonal = lax.psum(placed, 'row')  238 us
    ppermute x4, waiting for transfers between devices, from_partner(): return lax.ppermute(block, axis, route)  229 us
    psum x2, waiting for transfers between devices, broadcast(): return lax.psum(kept, axis)  169 us
    dot_general x5, matrix products, times_transposed(): lax.dot_general(left, right, (((1,), (1,)), ((), ())), precision=lax.Prec...  152 us
    another operation x7, other arithmetic, factor_panel(): jax.scipy.linalg.solve_triangular(low_factor, identity, lower=True)  122 us
  transfers between devices with their start and end apart: 15, of which 15 were waited for; matrix products, arithmetic and copies ran while one was open for 1% of the time, Pallas kernels for 0%

profile of v1, /device:TPU:0, one launch (start us, length us, event | category | flops | bytes accessed | tf_op | source)
XLA Modules:
  0.0 1829.9 jit_solution(8755437384180130347)
XLA Ops:
  6.5 23.0 %copy.106 = f32[2048,4096]{1,0:T(8,128)} copy(f32[2048,4096]{1,0:T(8,128)} %param.24) | data formatting | bytes 67108864
  32.8 81.1 %all-reduce.7.cloned.1.call-done = f32[512,512]{0,1:T(8,128)} async-done(((f32[512,512]{0,1:T(8,128)}), f32[512,512]{0,1:T(8,128)}) %all-reduce.7.cloned.1.call-update) | async-done | bytes 1048592 | tf_op jit(solution)/shard_map/psum | solution.py:79
  118.1 11.7 cholesky.374
  130.0 9.8 custom-call.31
  140.5 11.7 cholesky.393
  152.3 10.0 custom-call.32
  163.0 11.7 cholesky.414
  174.7 9.8 custom-call.33
  185.1 11.7 cholesky.431
  196.9 10.6 compare_reduce_fusion.9
  212.7 8.1 while.16
  220.8 39.3 %custom-call.34 = f32[4,128,128]{1,2,0:T(8,128)S(1)} custom-call(f32[4,128,128]{2,1,0:T(8,128)S(1)} %get-tuple-element.139), custom_call_target="InvertDiagBlocksLowerTriangular" | custom-call | tf_op jit(solution)/shard_map/jit(_solve_triangular)/triangular_solve | solution.py:82
  264.9 10.6 broadcast_select_fusion.1
  275.6 84.3 %all-reduce.9.cloned.1.call-done = f32[2048,512]{1,0:T(8,128)} async-done(((f32[2048,512]{1,0:T(8,128)}), f32[2048,512]{1,0:T(8,128)}) %all-reduce.9.cloned.1.call-update) | async-done | bytes 4194320 | tf_op jit(solution)/shard_map/psum | solution.py:24
  367.2 90.7 %collective-permute-done = f32[2,512,512]{2,1,0:T(8,128)S(1)} collective-permute-done((f32[2,512,512]{2,1,0:T(8,128)}, f32[2,512,512]{2,1,0:T(8,128)S(1)}, u32[]{:S(2)}, u32[]{:S(2)}) %collective-permute-start) | collective-permute-done | bytes 2097184 | tf_op jit(solution)/shard_map/ppermute | solution.py:34
  463.1 23.9 %collective-permute-done.1 = f32[1,512,512]{2,1,0:T(8,128)} collective-permute-done((f32[1,512,512]{2,1,0:T(8,128)}, f32[1,512,512]{2,1,0:T(8,128)}, u32[]{:S(2)}, u32[]{:S(2)}) %collective-permute-start.1) | collective-permute-done | bytes 1048608 | tf_op jit(solution)/shard_map/ppermute | solution.py:34
  489.7 23.4 %collective-permute-done.2 = f32[512,512]{1,0:T(8,128)} collective-permute-done((f32[512,512]{1,0:T(8,128)}, f32[512,512]{1,0:T(8,128)}, u32[]{:S(2)}, u32[]{:S(2)}) %collective-permute-start.2) | collective-permute-done | bytes 1048608 | tf_op jit(solution)/shard_map/ppermute | solution.py:14
  517.3 45.0 %collective-permute-done.3 = f32[1024,512]{1,0:T(8,128)} collective-permute-done((f32[1024,512]{1,0:T(8,128)S(1)}, f32[1024,512]{1,0:T(8,128)}, u32[]{:S(2)}, u32[]{:S(2)}) %collective-permute-start.3) | collective-permute-done | bytes 2097184 | tf_op jit(solution)/shard_map/ppermute | solution.py:14
  583.4 169.2 %collective-permute-done.4 = f32[2048,512]{1,0:T(8,128)} collective-permute-done((f32[2048,512]{1,0:T(8,128)}, f32[2048,512]{1,0:T(8,128)}, u32[]{:S(2)}, u32[]{:S(2)}) %collective-permute-start.4) | collective-permute-done | bytes 4194336 | tf_op jit(solution)/shard_map/ppermute | solution.py:14
  761.2 60.7 %subtract_select_fusion.1 = f32[2048,4096]{1,0:T(8,128)} fusion(f32[2048,4096]{1,0:T(8,128)} %fusion, pred[4096]{0:T(1024)(128)(4,1)S(1)} %broadcast_compare_fusion.1, pred[2048]{0:T(1024)(128)(4,1)S(1)} %get-tuple-element.222, f32[2048,512]{1,0:T(8,128)S(1)} %copy-done, f32[4096,512]{1,0:T(8,128)S(1)} %bitcast.183), kind=kOutput, calls=%fused_computation.7 | convolution fusion | flops 51564773376 | bytes 79697920 | tf_op jit(solution)/shard_map/dot_general | solution.py:43
  825.1 78.1 %all-reduce.11.cloned.1.call-done = f32[512,512]{0,1:T(8,128)} async-done(((f32[512,512]{0,1:T(8,128)}), f32[512,512]{0,1:T(8,128)}) %all-reduce.11.cloned.1.call-update) | async-done | bytes 1048592 | tf_op jit(solution)/shard_map/psum | solution.py:79
  906.1 11.7 cholesky.446
  918.0 9.8 custom-call.35
  928.5 11.7 cholesky.465
  940.3 10.0 custom-call.36
  950.9 11.7 cholesky.486
  962.7 9.8 custom-call.37
  973.1 11.7 cholesky.503
  991.7 8.1 while.17
  999.9 39.3 %custom-call.38 = f32[4,128,128]{1,2,0:T(8,128)S(1)} custom-call(f32[4,128,128]{2,1,0:T(8,128)S(1)} %get-tuple-element.140), custom_call_target="InvertDiagBlocksLowerTriangular" | custom-call | tf_op jit(solution)/shard_map/jit(_solve_triangular)/triangular_solve | solution.py:82
  1044.0 10.6 broadcast_select_fusion
  1054.8 85.0 %all-reduce.13.cloned.1.call-done = f32[2048,512]{1,0:T(8,128)} async-done(((f32[2048,512]{1,0:T(8,128)}), f32[2048,512]{1,0:T(8,128)}) %all-reduce.13.cloned.1.call-update) | async-done | bytes 4194320 | tf_op jit(solution)/shard_map/psum | solution.py:24
  1145.1 90.5 %collective-permute-done.5 = f32[2,512,512]{2,1,0:T(8,128)S(1)} collective-permute-done((f32[2,512,512]{2,1,0:T(8,128)S(1)}, f32[2,512,512]{2,1,0:T(8,128)S(1)}, u32[]{:S(2)}, u32[]{:S(2)}) %collective-permute-start.5) | collective-permute-done | bytes 2097184 | tf_op jit(solution)/shard_map/ppermute | solution.py:34
  1236.8 23.7 %collective-permute-done.6 = f32[1,512,512]{2,1,0:T(8,128)S(1)} collective-permute-done((f32[1,512,512]{2,1,0:T(8,128)S(1)}, f32[1,512,512]{2,1,0:T(8,128)S(1)}, u32[]{:S(2)}, u32[]{:S(2)}) %collective-permute-start.6) | collective-permute-done | bytes 1048608 | tf_op jit(solution)/shard_map/ppermute | solution.py:34
  1262.4 21.8 %collective-permute-done.7 = f32[512,512]{1,0:T(8,128)S(1)} collective-permute-done((f32[512,512]{1,0:T(8,128)S(1)}, f32[512,512]{1,0:T(8,128)S(1)}, u32[]{:S(2)}, u32[]{:S(2)}) %collective-permute-start.7) | collective-permute-done | bytes 1048608 | tf_op jit(solution)/shard_map/ppermute | solution.py:14
  1286.9 44.1 %collective-permute-done.8 = f32[1024,512]{1,0:T(8,128)S(1)} collective-permute-done((f32[1024,512]{1,0:T(8,128)S(1)}, f32[1024,512]{1,0:T(8,128)S(1)}, u32[]{:S(2)}, u32[]{:S(2)}) %collective-permute-start.8) | collective-permute-done | bytes 2097184 | tf_op jit(solution)/shard_map/ppermute | solution.py:14
  1345.6 170.8 %collective-permute-done.9 = f32[2048,512]{1,0:T(8,128)} collective-permute-done((f32[2048,512]{1,0:T(8,128)}, f32[2048,512]{1,0:T(8,128)}, u32[]{:S(2)}, u32[]{:S(2)}) %collective-permute-start.9) | collective-permute-done | bytes 4194336 | tf_op jit(solution)/shard_map/ppermute | solution.py:14
  1525.0 61.1 %subtract_select_fusion = f32[2048,4096]{1,0:T(8,128)} fusion(f32[2048,4096]{1,0:T(8,128)} %fusion.1, pred[4096]{0:T(1024)(128)(4,1)S(1)} %broadcast_compare_fusion, pred[2048]{0:T(1024)(128)(4,1)S(1)} %compare_and_fusion.1, f32[2048,512]{1,0:T(8,128)S(1)} %copy-done.1, f32[4096,512]{1,0:T(8,128)S(1)} %bitcast.184), kind=kOutput, calls=%fused_computation.6 | convolution fusion | flops 51564773376 | bytes 79697920 | tf_op jit(solution)/shard_map/dot_general | solution.py:43
  1589.1 78.6 %all-reduce.15.cloned.1.call-done = f32[512,512]{0,1:T(8,128)} async-done(((f32[512,512]{0,1:T(8,128)}), f32[512,512]{0,1:T(8,128)}) %all-reduce.15.cloned.1.call-update) | async-done | bytes 1048592 | tf_op jit(solution)/shard_map/psum | solution.py:79
  1670.6 11.7 cholesky.518
  1682.5 9.8 custom-call.39
  1693.0 11.7 cholesky.537
  1704.7 9.9 custom-call.40
  1715.4 11.7 cholesky.558
  1727.1 9.8 custom-call.41
  1737.5 11.9 cholesky.575
  1764.1 39.3 %custom-call.42 = f32[4,128,128]{1,2,0:T(8,128)S(1)} custom-call(f32[4,128,128]{2,1,0:T(8,128)S(1)} %get-tuple-element.141), custom_call_target="InvertDiagBlocksLowerTriangular" | custom-call | tf_op jit(solution)/shard_map/jit(_solve_triangular)/triangular_solve | solution.py:82
  1808.3 8.7 fusion.14
  (211 shorter events, 172.9 us)
Async XLA Ops:
  6.5 107.3 %all-reduce.7.cloned.1.call-start = ((), (), s32[]{:S(2)}) async-start(), calls=%async_computation | async-start | bytes 2097152 | tf_op jit(solution)/shard_map/psum | solution.py:79
  32.6 327.3 %all-reduce.9.cloned.1.call-start = ((), (), s32[]{:S(2)}) async-start(), calls=%async_computation.1 | async-start | bytes 8388608 | tf_op jit(solution)/shard_map/psum | solution.py:24
  113.9 2.8 copy-start.2
  275.6 627.6 %all-reduce.11.cloned.1.call-start = ((), (), s32[]{:S(2)}) async-start(), calls=%async_computation.2 | async-start | bytes 2097152 | tf_op jit(solution)/shard_map/psum | solution.py:79
  364.8 93.1 %collective-permute-start = (f32[2,512,512]{2,1,0:T(8,128)}, f32[2,512,512]{2,1,0:T(8,128)S(1)}, u32[]{:S(2)}, u32[]{:S(2)}) collective-permute-start(f32[2,512,512]{2,1,0:T(8,128)} %bitcast.13), channel_id=1, source_target_pairs={{0,16},{16,0},{4,20},{20,4},{8,24},{24,8},{12,28},{28,12},{1,17},{... | collective-permute-start | bytes 6291464 | tf_op jit(solution)/shard_map/ppermute | solution.py:34
  457.9 1.3 copy-start.7
  462.5 24.5 %collective-permute-start.1 = (f32[1,512,512]{2,1,0:T(8,128)}, f32[1,512,512]{2,1,0:T(8,128)}, u32[]{:S(2)}, u32[]{:S(2)}) collective-permute-start(f32[1,512,512]{2,1,0:T(8,128)} %slice_select_fusion.5), channel_id=1, source_target_pairs={{0,8},{8,0},{4,12},{12,4},{16,24},{24,16},{20,28},{28,20},{1,9},{9... | collective-permute-start | bytes 3145736 | tf_op jit(solution)/shard_map/ppermute | solution.py:34
  488.3 24.8 %collective-permute-start.2 = (f32[512,512]{1,0:T(8,128)}, f32[512,512]{1,0:T(8,128)}, u32[]{:S(2)}, u32[]{:S(2)}) collective-permute-start(f32[512,512]{1,0:T(8,128)} %select_bitcast_fusion.2), channel_id=1, source_target_pairs={{0,4},{4,0},{8,12},{12,8},{16,20},{20,16},{24,28},{28,24},{1,5},{5... | collective-permute-start | bytes 3145736 | tf_op jit(solution)/shard_map/ppermute | solution.py:14
  516.0 46.3 %collective-permute-start.3 = (f32[1024,512]{1,0:T(8,128)S(1)}, f32[1024,512]{1,0:T(8,128)}, u32[]{:S(2)}, u32[]{:S(2)}) collective-permute-start(f32[1024,512]{1,0:T(8,128)S(1)} %maximum_select_fusion.4), channel_id=1, source_target_pairs={{0,8},{4,12},{8,0},{12,4},{16,24},{20,28},{24,16},{28,20},{1,9},{5... | collective-permute-start | bytes 6291464 | tf_op jit(solution)/shard_map/ppermute | solution.py:14
  567.5 185.1 %collective-permute-start.4 = (f32[2048,512]{1,0:T(8,128)}, f32[2048,512]{1,0:T(8,128)}, u32[]{:S(2)}, u32[]{:S(2)}) collective-permute-start(f32[2048,512]{1,0:T(8,128)} %maximum_select_fusion.2), channel_id=1, source_target_pairs={{0,16},{4,20},{8,24},{12,28},{16,0},{20,4},{24,8},{28,12},{1,17},{... | collective-permute-start | bytes 12582920 | tf_op jit(solution)/shard_map/ppermute | solution.py:14
  759.0 2.2 copy-start
  824.9 315.0 %all-reduce.13.cloned.1.call-start = ((), (), s32[]{:S(2)}) async-start(), calls=%async_computation.3 | async-start | bytes 8388608 | tf_op jit(solution)/shard_map/psum | solution.py:24
  903.2 1.5 copy-start.3
  1054.6 613.1 %all-reduce.15.cloned.1.call-start = ((), (), s32[]{:S(2)}) async-start(), calls=%async_computation.4 | async-start | bytes 2097152 | tf_op jit(solution)/shard_map/psum | solution.py:79
  1142.6 93.0 %collective-permute-start.5 = (f32[2,512,512]{2,1,0:T(8,128)S(1)}, f32[2,512,512]{2,1,0:T(8,128)S(1)}, u32[]{:S(2)}, u32[]{:S(2)}) collective-permute-start(f32[2,512,512]{2,1,0:T(8,128)S(1)} %bitcast.193), channel_id=1, source_target_pairs={{0,16},{16,0},{4,20},{20,4},{8,24},{24,8},{12,28},{28,12},{1,17},{... | collective-permute-start | bytes 6291464 | tf_op jit(solution)/shard_map/ppermute | solution.py:34
  1236.3 24.2 %collective-permute-start.6 = (f32[1,512,512]{2,1,0:T(8,128)S(1)}, f32[1,512,512]{2,1,0:T(8,128)S(1)}, u32[]{:S(2)}, u32[]{:S(2)}) collective-permute-start(f32[1,512,512]{2,1,0:T(8,128)S(1)} %slice_select_fusion.4), channel_id=1, source_target_pairs={{0,8},{8,0},{4,12},{12,4},{16,24},{24,16},{20,28},{28,20},{1,9},{9... | collective-permute-start | bytes 3145736 | tf_op jit(solution)/shard_map/ppermute | solution.py:34
  1260.9 23.4 %collective-permute-start.7 = (f32[512,512]{1,0:T(8,128)S(1)}, f32[512,512]{1,0:T(8,128)S(1)}, u32[]{:S(2)}, u32[]{:S(2)}) collective-permute-start(f32[512,512]{1,0:T(8,128)S(1)} %select_bitcast_fusion.1), channel_id=1, source_target_pairs={{0,4},{4,0},{8,12},{12,8},{16,20},{20,16},{24,28},{28,24},{1,5},{5... | collective-permute-start | bytes 3145736 | tf_op jit(solution)/shard_map/ppermute | solution.py:14
  1284.5 53.3 %copy-start.5 = (f32[512,512]{1,0:T(8,128)S(1)}, f32[512,512]{1,0:T(8,128)}, u32[]{:S(2)}) copy-start(f32[512,512]{1,0:T(8,128)} %get-tuple-element.169) | copy-start | bytes 3145732
  1284.5 46.5 %collective-permute-start.8 = (f32[1024,512]{1,0:T(8,128)S(1)}, f32[1024,512]{1,0:T(8,128)S(1)}, u32[]{:S(2)}, u32[]{:S(2)}) collective-permute-start(f32[1024,512]{1,0:T(8,128)S(1)} %maximum_select_fusion.5), channel_id=1, source_target_pairs={{0,8},{4,12},{8,0},{12,4},{16,24},{20,28},{24,16},{28,20},{1,9},{5... | collective-permute-start | bytes 6291464 | tf_op jit(solution)/shard_map/ppermute | solution.py:14
  1333.8 182.6 %collective-permute-start.9 = (f32[2048,512]{1,0:T(8,128)}, f32[2048,512]{1,0:T(8,128)}, u32[]{:S(2)}, u32[]{:S(2)}) collective-permute-start(f32[2048,512]{1,0:T(8,128)} %maximum_select_fusion.3), channel_id=1, source_target_pairs={{0,16},{4,20},{8,24},{12,28},{16,0},{20,4},{24,8},{28,12},{1,17},{... | collective-permute-start | bytes 12582920 | tf_op jit(solution)/shard_map/ppermute | solution.py:14
  1522.8 2.2 copy-start.1
  1667.7 1.5 copy-start.4
  1808.3 8.7 copy-start.6
Sparse Core Ops, SparseCore 0:
  32.7 81.0 all-reduce.6
  275.7 84.1 all-reduce.8
  825.0 78.1 all-reduce.10
  1054.7 85.0 all-reduce.12
  1589.2 78.4 all-reduce.14
